TPU v7x, 512 devices: a whole 4x8x8 slice. The times are simulated.
512 devices in a mesh: seq: 16 (over z, core), mlp: 8 (over y), tp: 4 (over x).
Axes of the slice: x: 4, y: 8, z: 8, core: 2. Of those that a mesh axis runs over, the one named last changes fastest.
Arguments:
- hidden: bfloat16 [64, 2048], P('mlp'), may hold values from -6 to 6
- lengths: int32 [64], P('mlp'), may hold values from 4 to 8192, as said below
- attention_gain: bfloat16 [2048], replicated, may hold values from 0.099609375 to 1.8984375
- query_weight: bfloat16 [2048, 2048], P('seq', 'tp'), may hold values from -0.125 to 0.125
- key_weight: bfloat16 [2048, 512], P('seq', 'tp'), may hold values from -0.125 to 0.125
- value_weight: bfloat16 [2048, 512], P('seq', 'tp'), may hold values from -0.125 to 0.125
- cached_keys: bfloat16 [64, 8192, 512], P('mlp', 'seq', 'tp'), may hold values from -800 to 800
- cached_values: bfloat16 [64, 8192, 512], P('mlp', 'seq', 'tp'), may hold values from -8 to 8
- output_weight: bfloat16 [2048, 2048], P('tp', 'seq'), may hold values from -0.125 to 0.125
- feedforward_gain: bfloat16 [2048], replicated, may hold values from 0.099609375 to 1.8984375
- gate_weight: bfloat16 [2048, 8192], P('mlp', ('seq', 'tp')), may hold values from -0.125 to 0.125
- up_weight: bfloat16 [2048, 8192], P('mlp', ('seq', 'tp')), may hold values from -0.125 to 0.125
- down_weight: bfloat16 [8192, 2048], P(('seq', 'tp'), 'mlp'), may hold values from -0.0625 to 0.0625
Outputs:
- updated_hidden: bfloat16 [64, 2048], P('mlp')
- new_keys: bfloat16 [64, 512], P('mlp', 'tp')
- new_values: bfloat16 [64, 512], P('mlp', 'tp')
Inputs may be any that keep to these rules, and one draw needn't show every extreme that they name: `lengths`: one request in every draw has exactly 8192 cached tokens.
All inputs are finite; a program needn't handle non-finite values.
Results may differ from a plain program's by a relative error of at most 0.012.
Values may be sent and summed in bfloat16 or wider, within the bound.
No kernel may reach another device: no remote copies, remote signals or barrier semaphores. Data moves between devices by JAX's collectives and lax.ppermute only.
A program may use at most 64 MiB of HBM per device.

v0:
```python
import jax
import jax.numpy as jnp
from jax import lax
from jax.sharding import PartitionSpec as P

HD = 64


def rms_norm(vectors, weights):
    mean_square = jnp.mean(vectors * vectors, axis=-1, keepdims=True)
    return vectors * lax.rsqrt(mean_square + 1e-05) * weights.astype(jnp.float32)


def rotate(vectors, positions):
    half_dim = vectors.shape[-1] // 2
    inverse = 500000.0 ** (-(jnp.arange(half_dim, dtype=jnp.float32) * 2.0 / vectors.shape[-1]))
    angles = positions.astype(jnp.float32)[:, None] * inverse[None, :]
    cosine = jnp.cos(angles)[:, None, :]
    sine_part = jnp.sin(angles)[:, None, :]
    first_half = vectors[..., :half_dim]
    second_half = vectors[..., half_dim:]
    return jnp.concatenate(
        [
            first_half * cosine - second_half * sine_part,
            second_half * cosine + first_half * sine_part,
        ],
        axis=-1,
    )


def gathered_sum(x, axis):
    return jnp.sum(lax.all_gather(x, axis), axis=0)


def gather_blocks(x, axis):
    size = lax.axis_size(axis)
    me = lax.axis_index(axis)
    held = x[None]
    step = 1
    while step < size:
        other = lax.ppermute(held, axis, [(i, i ^ step) for i in range(size)])
        upper = me // step % 2 == 1
        held = jnp.where(
            upper, jnp.concatenate([other, held], axis=0), jnp.concatenate([held, other], axis=0)
        )
        step *= 2
    return held


def butterfly_sum(x, axis):
    size = lax.axis_size(axis)
    step = 1
    while step < size:
        pairs = [(i, i ^ step) for i in range(size)]
        x = x + lax.ppermute(x, axis, pairs)
        step *= 2
    return x


def per_device(
    hidden,
    lengths,
    attention_gain,
    query_weight,
    key_weight,
    value_weight,
    cached_keys,
    cached_values,
    output_weight,
    feedforward_gain,
    gate_weight,
    up_weight,
    down_weight,
):
    slab_rows, hidden_units = gate_weight.shape
    with jax.named_scope("mlp_weight_gather"):
        slab = jnp.stack(
            [gate_weight, up_weight, down_weight.reshape(slab_rows, hidden_units)], axis=0
        )
        blocks = gather_blocks(slab, "mlp")
    slabs = blocks.shape[0]
    gate_full = blocks[:, 0].reshape(slabs * slab_rows, hidden_units)
    up_full = blocks[:, 1].reshape(slabs * slab_rows, hidden_units)
    down_blocks = blocks[:, 2].reshape(slabs, hidden_units, slab_rows)
    requests = hidden.shape[0]
    stream = hidden.astype(jnp.float32)
    normed = rms_norm(stream, attention_gain).astype(jnp.bfloat16)
    column_width = query_weight.shape[0]
    own_columns = lax.dynamic_slice_in_dim(
        normed, lax.axis_index("seq") * column_width, column_width, 1
    )
    query_width = query_weight.shape[1]
    key_width = key_weight.shape[1]
    with jax.named_scope("qkv_projection"):
        partial = jnp.concatenate(
            [
                jnp.dot(own_columns, query_weight, preferred_element_type=jnp.float32),
                jnp.dot(own_columns, key_weight, preferred_element_type=jnp.float32),
                jnp.dot(own_columns, value_weight, preferred_element_type=jnp.float32),
            ],
            axis=1,
        )
        total = gathered_sum(partial, "seq")
    queries_raw = total[:, :query_width]
    keys_raw = total[:, query_width : query_width + key_width]
    values_raw = total[:, query_width + key_width :]
    local_heads = query_width // HD
    key_heads = key_width // HD
    group_size = local_heads // key_heads
    queries = rotate(queries_raw.reshape(requests, local_heads, HD), lengths).astype(jnp.bfloat16)
    new_keys = (
        rotate(keys_raw.reshape(requests, key_heads, HD), lengths)
        .reshape(requests, key_heads * HD)
        .astype(jnp.bfloat16)
    )
    new_values = values_raw.astype(jnp.bfloat16)
    grouped = queries.reshape(requests, key_heads, group_size, HD)
    block_span = cached_keys.shape[1]
    key_blocks = cached_keys.reshape(requests, block_span, key_heads, HD)
    value_blocks = cached_values.reshape(requests, block_span, key_heads, HD)
    score_scale = HD ** (-0.5)
    first_position = lax.axis_index("seq") * block_span
    positions = first_position + jnp.arange(block_span, dtype=jnp.int32)
    valid_mask = (positions[None, :] < lengths[:, None])[:, None, None, :]
    with jax.named_scope("local_attention"):
        scores = (
            jnp.einsum("rgqd,rpgd->rgqp", grouped, key_blocks, preferred_element_type=jnp.float32)
            * score_scale
        )
        block_max = jnp.max(jnp.where(valid_mask, scores, -1e30), axis=-1)
        exp_weights = jnp.where(valid_mask, jnp.exp(scores - block_max[..., None]), 0.0)
        block_sum = jnp.sum(exp_weights, axis=-1)
        block_acc = jnp.einsum(
            "rgqp,rpgd->rgqd",
            exp_weights.astype(jnp.bfloat16),
            value_blocks,
            preferred_element_type=jnp.float32,
        )
    with jax.named_scope("softmax_merge"):
        state = jnp.concatenate([block_max[..., None], block_sum[..., None], block_acc], axis=-1)
        every_state = lax.all_gather(state, "seq")
        every_max = every_state[..., 0]
        every_sum = every_state[..., 1]
        every_acc = every_state[..., 2:]
        query_float = grouped.astype(jnp.float32)
        self_score = (
            jnp.sum(
                query_float * new_keys.astype(jnp.float32).reshape(requests, key_heads, 1, HD),
                axis=-1,
            )
            * score_scale
        )
        overall_max = jnp.maximum(jnp.max(every_max, axis=0), self_score)
        rescale = jnp.exp(every_max - overall_max[None])
        self_weight = jnp.exp(self_score - overall_max)
        total_weight = jnp.sum(every_sum * rescale, axis=0) + self_weight
        weighted_sum = jnp.sum(every_acc * rescale[..., None], axis=0) + self_weight[
            ..., None
        ] * new_values.astype(jnp.float32).reshape(requests, key_heads, 1, HD)
        attended = (
            (weighted_sum / total_weight[..., None])
            .reshape(requests, local_heads * HD)
            .astype(jnp.bfloat16)
        )
    with jax.named_scope("output_projection"):
        partial_output = jnp.dot(attended, output_weight, preferred_element_type=jnp.float32)
        projected = lax.psum(partial_output, "tp").astype(jnp.bfloat16)
        projected = lax.all_gather(projected, "seq", axis=1, tiled=True)
    mixed_stream = stream + projected.astype(jnp.float32)
    mlp_input = rms_norm(mixed_stream, feedforward_gain).astype(jnp.bfloat16)
    with jax.named_scope("feed_forward"):
        gate = jnp.dot(mlp_input, gate_full, preferred_element_type=jnp.float32)
        upward = jnp.dot(mlp_input, up_full, preferred_element_type=jnp.float32)
        activated = (jax.nn.silu(gate) * upward).astype(jnp.bfloat16)
        down_part = jnp.einsum(
            "rh,jhc->rjc", activated, down_blocks, preferred_element_type=jnp.float32
        ).reshape(requests, slabs * slab_rows)
    with jax.named_scope("down_reduction"):
        down_total = butterfly_sum(gathered_sum(down_part, "tp"), "seq").astype(jnp.bfloat16)
    updated_hidden = (mixed_stream + down_total.astype(jnp.float32)).astype(jnp.bfloat16)
    return (updated_hidden, new_keys, new_values)


def solution(mesh):
    return jax.shard_map(
        per_device,
        mesh=mesh,
        in_specs=(
            P("mlp", None),
            P("mlp"),
            P(),
            P("seq", "tp"),
            P("seq", "tp"),
            P("seq", "tp"),
            P("mlp", "seq", "tp"),
            P("mlp", "seq", "tp"),
            P("tp", "seq"),
            P(),
            P("mlp", ("seq", "tp")),
            P("mlp", ("seq", "tp")),
            P(("seq", "tp"), "mlp"),
        ),
        out_specs=(P("mlp", None), P("mlp", "tp"), P("mlp", "tp")),
        check_vma=False,
    )
```

profile of v0, /device:TPU:64, one launch (start us, length us, event | category | flops | bytes accessed | tf_op | source)
XLA Modules:
  0.0 163.4 jit_solution(15652032731097320502)
XLA Ops:
  0.7 1.0 reshape.177
  1.6 0.9 maximum_bitcast_fusion
  2.5 3.5 %collective-permute-start = (bf16[1,3,256,128]{3,2,1,0:T(8,128)(2,1)S(1)}, bf16[1,3,256,128]{3,2,1,0:T(8,128)(2,1)}, u32[]{:S(2)}, u32[]{:S(2)}) collective-permute-start(bf16[1,3,256,128]{3,2,1,0:T(8,128)(2,1)S(1)} %maximum_bitcast_fusion), channel_id=1, source_target_pairs={{0,4},{4,0},{8,12},{12,8},{16,20},{20,16},{24,28},{28,24},{1,5},{5... | collective-permute-start | bytes 589832 | tf_op jit(solution)/shard_map/mlp_weight_gather/ppermute | solution.py:41
  6.0 0.8 convert_element_type.70
  6.8 0.9 multiply_reduce_fusion.1
  7.7 0.8 dynamic-slice
  8.5 0.2 fusion.26
  8.7 0.9 fusion.24
  9.6 1.0 fusion.28
  10.6 21.2 %all-gather = f32[128,768]{1,0:T(8,128)S(1)} all-gather(f32[8,768]{1,0:T(8,128)S(1)} %pad_maximum_fusion.1), channel_id=2, replica_groups=mesh['seq'=16,'mlp'=8,'tp'=4] {'seq'}, dimensions={0}, use_global_device_ids=true | all-gather | bytes 417792 | tf_op jit(solution)/shard_map/qkv_projection/all_gather | solution.py:32
  32.0 0.5 copy.107
  32.6 0.5 copy.110
  33.3 0.4 select_reduce_fusion
  33.7 0.2 fusion.2
  34.0 0.4 fusion.3
  34.4 0.2 copy.112
  34.6 0.2 copy.111
  34.9 18.2 %all-gather.1 = f32[128,2,4,66]{3,2,1,0:T(4,128)S(1)} all-gather(f32[8,2,4,66]{3,2,1,0:T(4,128)S(1)} %pad_maximum_fusion), channel_id=3, replica_groups=mesh['seq'=16,'mlp'=8,'tp'=4] {'seq'}, dimensions={0}, use_global_device_ids=true | all-gather | bytes 287232 | tf_op jit(solution)/shard_map/softmax_merge/all_gather | solution.py:141
  53.3 0.3 fusion.23
  53.5 0.3 slice-done
  54.1 0.2 multiply_reduce_fusion.2
  54.4 0.5 copy.119
  54.8 0.5 copy.127
  55.4 1.1 maximum_select_fusion.2
  56.6 4.5 %collective-permute-start.1 = (bf16[2,3,256,128]{3,2,1,0:T(8,128)(2,1)S(1)}, bf16[2,3,256,128]{3,2,1,0:T(8,128)(2,1)S(1)}, u32[]{:S(2)}, u32[]{:S(2)}) collective-permute-start(bf16[2,3,256,128]{3,2,1,0:T(8,128)(2,1)S(1)} %maximum_select_fusion.2), channel_id=1, source_target_pairs={{0,8},{4,12},{8,0},{12,4},{16,24},{20,28},{24,16},{28,20},{1,9},{5... | collective-permute-start | bytes 1179656 | tf_op jit(solution)/shard_map/mlp_weight_gather/ppermute | solution.py:41
  61.1 0.2 fusion.10
  61.5 0.3 fusion
  61.8 17.2 %collective-permute-done.1 = bf16[2,3,256,128]{3,2,1,0:T(8,128)(2,1)S(1)} collective-permute-done((bf16[2,3,256,128]{3,2,1,0:T(8,128)(2,1)S(1)}, bf16[2,3,256,128]{3,2,1,0:T(8,128)(2,1)S(1)}, u32[]{:S(2)}, u32[]{:S(2)}) %collective-permute-start.1) | collective-permute-done | bytes 393248 | tf_op jit(solution)/shard_map/mlp_weight_gather/ppermute | solution.py:41
  79.2 6.9 %collective-permute-start.2 = (bf16[4,3,256,128]{3,2,1,0:T(8,128)(2,1)S(1)}, bf16[4,3,256,128]{3,2,1,0:T(8,128)(2,1)S(1)}, u32[]{:S(2)}, u32[]{:S(2)}) collective-permute-start(bf16[4,3,256,128]{3,2,1,0:T(8,128)(2,1)S(1)} %maximum_select_fusion.1), channel_id=1, source_target_pairs={{0,16},{4,20},{8,24},{12,28},{16,0},{20,4},{24,8},{28,12},{1,17},{... | collective-permute-start | bytes 2359304 | tf_op jit(solution)/shard_map/mlp_weight_gather/ppermute | solution.py:41
  86.5 10.5 %psum.7 = bf16[8,128]{1,0:T(8,128)(2,1)S(1)} all-reduce(f32[8,128]{1,0:T(8,128)S(1)} %fusion.30), channel_id=1, replica_groups=mesh['seq'=16,'mlp'=8,'tp'=4] {'tp'}, use_global_device_ids=true, to_apply=%region_8.9 | all-reduce | flops 1024 | bytes 6144 | tf_op jit(solution)/shard_map/output_projection/psum | solution.py:167
  96.9 14.5 %all_gather.22 = bf16[8,2048]{1,0:T(8,128)(2,1)S(1)} all-gather(bf16[8,128]{1,0:T(8,128)(2,1)S(1)} %psum.7), channel_id=1, replica_groups=mesh['seq'=16,'mlp'=8,'tp'=4] {'seq'}, dimensions={1}, use_global_device_ids=true | all-gather | bytes 34816 | tf_op jit(solution)/shard_map/output_projection/all_gather | solution.py:168
  111.6 9.9 %collective-permute-done.2 = bf16[4,3,256,128]{3,2,1,0:T(8,128)(2,1)S(1)} collective-permute-done((bf16[4,3,256,128]{3,2,1,0:T(8,128)(2,1)S(1)}, bf16[4,3,256,128]{3,2,1,0:T(8,128)(2,1)S(1)}, u32[]{:S(2)}, u32[]{:S(2)}) %collective-permute-start.2) | collective-permute-done | bytes 786464 | tf_op jit(solution)/shard_map/mlp_weight_gather/ppermute | solution.py:41
  121.5 0.2 maximum_select_fusion
  121.9 0.2 reshape_squeeze.11
  122.0 0.3 copy.121
  122.3 0.2 fusion.19
  122.6 0.4 fusion.13
  123.0 12.6 %all-gather.2 = f32[32,2048]{1,0:T(8,128)S(1)} all-gather(f32[8,2048]{1,0:T(8,128)S(1)} %fusion.13), channel_id=4, replica_groups=mesh['seq'=16,'mlp'=8,'tp'=4] {'tp'}, dimensions={0}, use_global_device_ids=true | all-gather | bytes 327680 | tf_op jit(solution)/shard_map/down_reduction/all_gather | solution.py:32
  135.6 1.9 %collective-permute-start.3 = (f32[8,2048]{1,0:T(8,128)S(1)}, f32[8,2048]{1,0:T(8,128)S(1)}, u32[]{:S(2)}, u32[]{:S(2)}) collective-permute-start(f32[8,2048]{1,0:T(8,128)S(1)} %bitcast_reduce_fusion.1), channel_id=1, source_target_pairs={{0,32},{32,0},{64,96},{96,64},{128,160},{160,128},{192,224},{224,1... | collective-permute-start | bytes 196616 | tf_op jit(solution)/shard_map/down_reduction/ppermute | solution.py:55
  137.6 1.2 collective-permute-done.3
  138.8 2.3 %collective-permute-start.4 = (f32[8,2048]{1,0:T(8,128)S(1)}, f32[8,2048]{1,0:T(8,128)S(1)}, u32[]{:S(2)}, u32[]{:S(2)}) collective-permute-start(f32[8,2048]{1,0:T(8,128)S(1)} %add.98), channel_id=1, source_target_pairs={{0,64},{32,96},{64,0},{96,32},{128,192},{160,224},{192,128},{224,1... | collective-permute-start | bytes 196616 | tf_op jit(solution)/shard_map/down_reduction/ppermute | solution.py:55
  141.1 3.9 %collective-permute-done.4 = f32[8,2048]{1,0:T(8,128)S(1)} collective-permute-done((f32[8,2048]{1,0:T(8,128)S(1)}, f32[8,2048]{1,0:T(8,128)S(1)}, u32[]{:S(2)}, u32[]{:S(2)}) %collective-permute-start.4) | collective-permute-done | bytes 65568 | tf_op jit(solution)/shard_map/down_reduction/ppermute | solution.py:55
  145.0 2.2 %collective-permute-start.5 = (f32[8,2048]{1,0:T(8,128)S(1)}, f32[8,2048]{1,0:T(8,128)S(1)}, u32[]{:S(2)}, u32[]{:S(2)}) collective-permute-start(f32[8,2048]{1,0:T(8,128)S(1)} %add.99), channel_id=1, source_target_pairs={{0,128},{32,160},{64,192},{96,224},{128,0},{160,32},{192,64},{224,... | collective-permute-start | bytes 196616 | tf_op jit(solution)/shard_map/down_reduction/ppermute | solution.py:55
  147.1 4.9 %collective-permute-done.5 = f32[8,2048]{1,0:T(8,128)S(1)} collective-permute-done((f32[8,2048]{1,0:T(8,128)S(1)}, f32[8,2048]{1,0:T(8,128)S(1)}, u32[]{:S(2)}, u32[]{:S(2)}) %collective-permute-start.5) | collective-permute-done | bytes 65568 | tf_op jit(solution)/shard_map/down_reduction/ppermute | solution.py:55
  152.0 3.4 %collective-permute-start.6 = (f32[8,2048]{1,0:T(8,128)S(1)}, f32[8,2048]{1,0:T(8,128)S(1)}, u32[]{:S(2)}, u32[]{:S(2)}) collective-permute-start(f32[8,2048]{1,0:T(8,128)S(1)} %add.100), channel_id=1, source_target_pairs={{0,256},{32,288},{64,320},{96,352},{128,384},{160,416},{192,448},{... | collective-permute-start | bytes 196616 | tf_op jit(solution)/shard_map/down_reduction/ppermute | solution.py:55
  155.4 0.7 convert_element_type.88
  156.1 6.7 %collective-permute-done.6 = f32[8,2048]{1,0:T(8,128)S(1)} collective-permute-done((f32[8,2048]{1,0:T(8,128)S(1)}, f32[8,2048]{1,0:T(8,128)S(1)}, u32[]{:S(2)}, u32[]{:S(2)}) %collective-permute-start.6) | collective-permute-done | bytes 65568 | tf_op jit(solution)/shard_map/down_reduction/ppermute | solution.py:55
  162.8 0.6 add_convert_fusion
  (59 shorter events, 2.0 us)
Async XLA Ops:
  0.6 7.8 %copy-start = (bf16[128,512]{1,0:T(8,128)(2,1)S(1)}, bf16[128,512]{1,0:T(8,128)(2,1)}, u32[]{:S(2)}) copy-start(bf16[128,512]{1,0:T(8,128)(2,1)} %param.16) | copy-start | bytes 393220
  0.6 31.3 %copy-start.9 = (s32[8]{0:T(128)S(1)}, s32[8]{0:T(128)}, u32[]{:S(2)}) copy-start(s32[8]{0:T(128)} %param.14) | copy-start | bytes 100
  0.7 31.4 %copy-start.2 = (bf16[8,512,128]{2,1,0:T(8,128)(2,1)S(1)}, bf16[8,512,128]{2,1,0:T(8,128)(2,1)}, u32[]{:S(2)}) copy-start(bf16[8,512,128]{2,1,0:T(8,128)(2,1)} %param.19) | copy-start | bytes 3145732
  2.5 52.9 %collective-permute-start = (bf16[1,3,256,128]{3,2,1,0:T(8,128)(2,1)S(1)}, bf16[1,3,256,128]{3,2,1,0:T(8,128)(2,1)}, u32[]{:S(2)}, u32[]{:S(2)}) collective-permute-start(bf16[1,3,256,128]{3,2,1,0:T(8,128)(2,1)S(1)} %maximum_bitcast_fusion), channel_id=1, source_target_pairs={{0,4},{4,0},{8,12},{12,8},{16,20},{20,16},{24,28},{28,24},{1,5},{5... | collective-permute-start | bytes 589832 | tf_op jit(solution)/shard_map/mlp_weight_gather/ppermute | solution.py:41
  9.6 23.0 %copy-start.3 = (bf16[8,512,128]{2,1,0:T(8,128)(2,1)S(1)}, bf16[8,512,128]{2,1,0:T(8,128)(2,1)}, u32[]{:S(2)}) copy-start(bf16[8,512,128]{2,1,0:T(8,128)(2,1)} %param.20) | copy-start | bytes 3145732
  31.8 1.3 copy-start.5
  53.2 0.7 slice-start
  53.8 7.4 %copy-start.6 = (f32[8,768]{1,0:T(8,128)S(1)}, f32[8,768]{1,0:T(8,128)}, u32[]{:S(2)}) copy-start(f32[8,768]{1,0:T(8,128)} %copy-done.5) | copy-start | bytes 73732
  55.4 30.9 %copy-start.8 = (bf16[2048]{0:T(1024)(128)(2,1)S(1)}, bf16[2048]{0:T(1024)(128)(2,1)}, u32[]{:S(2)}) copy-start(bf16[2048]{0:T(1024)(128)(2,1)} %param.22) | copy-start | bytes 12292
  55.4 30.9 %copy-start.4 = (bf16[512,128]{1,0:T(8,128)(2,1)S(1)}, bf16[512,128]{1,0:T(8,128)(2,1)}, u32[]{:S(2)}) copy-start(bf16[512,128]{1,0:T(8,128)(2,1)} %param.21) | copy-start | bytes 393220
  56.5 54.9 %copy-start.1 = (bf16[8,2048]{1,0:T(8,128)(2,1)S(1)}, bf16[8,2048]{1,0:T(8,128)(2,1)}, u32[]{:S(2)}) copy-start(bf16[8,2048]{1,0:T(8,128)(2,1)} %param.13) | copy-start | bytes 98308
  56.6 22.5 %collective-permute-start.1 = (bf16[2,3,256,128]{3,2,1,0:T(8,128)(2,1)S(1)}, bf16[2,3,256,128]{3,2,1,0:T(8,128)(2,1)S(1)}, u32[]{:S(2)}, u32[]{:S(2)}) collective-permute-start(bf16[2,3,256,128]{3,2,1,0:T(8,128)(2,1)S(1)} %maximum_select_fusion.2), channel_id=1, source_target_pairs={{0,8},{4,12},{8,0},{12,4},{16,24},{20,28},{24,16},{28,20},{1,9},{5... | collective-permute-start | bytes 1179656 | tf_op jit(solution)/shard_map/mlp_weight_gather/ppermute | solution.py:41
  61.3 60.5 %copy-start.7 = (bf16[8,128]{1,0:T(8,128)(2,1)}, bf16[8,128]{1,0:T(8,128)(2,1)S(1)}, u32[]{:S(2)}) copy-start(bf16[8,128]{1,0:T(8,128)(2,1)S(1)} %slice.79) | copy-start | bytes 6148
  79.2 42.3 %collective-permute-start.2 = (bf16[4,3,256,128]{3,2,1,0:T(8,128)(2,1)S(1)}, bf16[4,3,256,128]{3,2,1,0:T(8,128)(2,1)S(1)}, u32[]{:S(2)}, u32[]{:S(2)}) collective-permute-start(bf16[4,3,256,128]{3,2,1,0:T(8,128)(2,1)S(1)} %maximum_select_fusion.1), channel_id=1, source_target_pairs={{0,16},{4,20},{8,24},{12,28},{16,0},{20,4},{24,8},{28,12},{1,17},{... | collective-permute-start | bytes 2359304 | tf_op jit(solution)/shard_map/mlp_weight_gather/ppermute | solution.py:41
  135.6 3.1 %collective-permute-start.3 = (f32[8,2048]{1,0:T(8,128)S(1)}, f32[8,2048]{1,0:T(8,128)S(1)}, u32[]{:S(2)}, u32[]{:S(2)}) collective-permute-start(f32[8,2048]{1,0:T(8,128)S(1)} %bitcast_reduce_fusion.1), channel_id=1, source_target_pairs={{0,32},{32,0},{64,96},{96,64},{128,160},{160,128},{192,224},{224,1... | collective-permute-start | bytes 196616 | tf_op jit(solution)/shard_map/down_reduction/ppermute | solution.py:55
  138.8 6.2 %collective-permute-start.4 = (f32[8,2048]{1,0:T(8,128)S(1)}, f32[8,2048]{1,0:T(8,128)S(1)}, u32[]{:S(2)}, u32[]{:S(2)}) collective-permute-start(f32[8,2048]{1,0:T(8,128)S(1)} %add.98), channel_id=1, source_target_pairs={{0,64},{32,96},{64,0},{96,32},{128,192},{160,224},{192,128},{224,1... | collective-permute-start | bytes 196616 | tf_op jit(solution)/shard_map/down_reduction/ppermute | solution.py:55
  145.0 7.1 %collective-permute-start.5 = (f32[8,2048]{1,0:T(8,128)S(1)}, f32[8,2048]{1,0:T(8,128)S(1)}, u32[]{:S(2)}, u32[]{:S(2)}) collective-permute-start(f32[8,2048]{1,0:T(8,128)S(1)} %add.99), channel_id=1, source_target_pairs={{0,128},{32,160},{64,192},{96,224},{128,0},{160,32},{192,64},{224,... | collective-permute-start | bytes 196616 | tf_op jit(solution)/shard_map/down_reduction/ppermute | solution.py:55
  152.0 10.8 %collective-permute-start.6 = (f32[8,2048]{1,0:T(8,128)S(1)}, f32[8,2048]{1,0:T(8,128)S(1)}, u32[]{:S(2)}, u32[]{:S(2)}) collective-permute-start(f32[8,2048]{1,0:T(8,128)S(1)} %add.100), channel_id=1, source_target_pairs={{0,256},{32,288},{64,320},{96,352},{128,384},{160,416},{192,448},{... | collective-permute-start | bytes 196616 | tf_op jit(solution)/shard_map/down_reduction/ppermute | solution.py:55
where the time goes:
time: 164 us; the launch traced here: 163 us
  blocking collectives  77 us (47%)
  waiting for transfers between devices  43.8 us (27%)
  starting transfers between devices  24.6 us (15%)
  other arithmetic  6.82 us (4%)
  local copies, waits for them, and re-layouts  6.29 us (4%)
  matrix products  3.79 us (2%)
    all_gather x2, blocking collectives, gathered_sum(): return jnp.sum(lax.all_gather(x, axis), axis=0)  33.8 us
    ppermute x3, waiting for transfers between devices, gather_blocks(): other = lax.ppermute(held, axis, [(i, i ^ step) for i in range(size)])  27.1 us
    all_gather x1, blocking collectives, per_device(): every_state = lax.all_gather(state, 'seq')  18.2 us
    ppermute x4, waiting for transfers between devices, butterfly_sum(): x = x + lax.ppermute(x, axis, pairs)  16.8 us
    ppermute x3, starting transfers between devices, gather_blocks(): other = lax.ppermute(held, axis, [(i, i ^ step) for i in range(size)])  14.9 us
    all_gather x1, blocking collectives, per_device(): projected = lax.all_gather(projected, 'seq', axis=1, tiled=True)  14.5 us
    psum x1, blocking collectives, per_device(): projected = lax.psum(partial_output, 'tp').astype(jnp.bfloat16)  10.5 us
    ppermute x4, starting transfers between devices, butterfly_sum(): x = x + lax.ppermute(x, axis, pairs)  9.69 us
  transfers between devices with their start and end apart: 7, of which 6 were waited for; matrix products, arithmetic and copies ran while one was open for 7% of the time, Pallas kernels for 0%

commit v1 on v0

--- a/solution.py
+++ b/solution.py
@@ -164,7 +164,7 @@
         )
     with jax.named_scope("output_projection"):
         partial_output = jnp.dot(attended, output_weight, preferred_element_type=jnp.float32)
-        projected = lax.psum(partial_output, "tp").astype(jnp.bfloat16)
+        projected = jnp.sum(lax.all_gather(partial_output, "tp"), axis=0).astype(jnp.bfloat16)
         projected = lax.all_gather(projected, "seq", axis=1, tiled=True)
     mixed_stream = stream + projected.astype(jnp.float32)
     mlp_input = rms_norm(mixed_stream, feedforward_gain).astype(jnp.bfloat16)

time: 164 us -> 164 us (level)
  blocking collectives: 77 us -> 78.9 us
  waiting for transfers between devices: 43.8 us -> 41.9 us
    all_gather x0 -> x1, blocking collectives: none -> 12.4 us  [per_device(): lax.all_gather(partial_output, 'tp')]
    psum x1 -> x0, blocking collectives: 10.5 us -> none  [per_device(): projected = lax.psum(partial_output, 'tp').astype(jnp.bfloat16)]
    ppermute x3, waiting for transfers between devices: 27.1 us -> 25.2 us  [gather_blocks(): other = lax.ppermute(held, axis, [(i, i ^ step) for i in range(size)])]
where the time goes in v1:
time: 164 us; the launch traced here: 163 us
  blocking collectives  78.9 us (48%)
  waiting for transfers between devices  41.9 us (26%)
  starting transfers between devices  24.6 us (15%)
  other arithmetic  6.83 us (4%)
  local copies, waits for them, and re-layouts  6.29 us (4%)
  matrix products  3.79 us (2%)
    all_gather x2, blocking collectives, gathered_sum(): return jnp.sum(lax.all_gather(x, axis), axis=0)  33.8 us
    ppermute x3, waiting for transfers between devices, gather_blocks(): other = lax.ppermute(held, axis, [(i, i ^ step) for i in range(size)])  25.2 us
    all_gather x1, blocking collectives, per_device(): every_state = lax.all_gather(state, 'seq')  18.2 us
    ppermute x4, waiting for transfers between devices, butterfly_sum(): x = x + lax.ppermute(x, axis, pairs)  16.8 us
    ppermute x3, starting transfers between devices, gather_blocks(): other = lax.ppermute(held, axis, [(i, i ^ step) for i in range(size)])  14.9 us
    all_gather x1, blocking collectives, per_device(): projected = lax.all_gather(projected, 'seq', axis=1, tiled=True)  14.5 us
    all_gather x1, blocking collectives, per_device(): lax.all_gather(partial_output, 'tp')  12.4 us
    ppermute x4, starting transfers between devices, butterfly_sum(): x = x + lax.ppermute(x, axis, pairs)  9.69 us
  transfers between devices with their start and end apart: 7, of which 6 were waited for; matrix products, arithmetic and copies ran while one was open for 7% of the time, Pallas kernels for 0%

profile of v1, /device:TPU:64, one launch (start us, length us, event | category | flops | bytes accessed | tf_op | source)
XLA Modules:
  0.0 163.4 jit_solution(13436895314683782846)
XLA Ops:
  0.7 1.0 reshape.177
  1.6 0.9 maximum_bitcast_fusion
  2.5 3.5 %collective-permute-start = (bf16[1,3,256,128]{3,2,1,0:T(8,128)(2,1)S(1)}, bf16[1,3,256,128]{3,2,1,0:T(8,128)(2,1)}, u32[]{:S(2)}, u32[]{:S(2)}) collective-permute-start(bf16[1,3,256,128]{3,2,1,0:T(8,128)(2,1)S(1)} %maximum_bitcast_fusion), channel_id=1, source_target_pairs={{0,4},{4,0},{8,12},{12,8},{16,20},{20,16},{24,28},{28,24},{1,5},{5... | collective-permute-start | bytes 589832 | tf_op jit(solution)/shard_map/mlp_weight_gather/ppermute | solution.py:41
  6.0 0.8 convert_element_type.70
  6.8 0.9 multiply_reduce_fusion.1
  7.7 0.8 dynamic-slice
  8.5 0.2 fusion.26
  8.7 0.9 fusion.24
  9.6 1.0 fusion.28
  10.6 21.2 %all-gather = f32[128,768]{1,0:T(8,128)S(1)} all-gather(f32[8,768]{1,0:T(8,128)S(1)} %pad_maximum_fusion.1), channel_id=2, replica_groups=mesh['seq'=16,'mlp'=8,'tp'=4] {'seq'}, dimensions={0}, use_global_device_ids=true | all-gather | bytes 417792 | tf_op jit(solution)/shard_map/qkv_projection/all_gather | solution.py:32
  32.0 0.5 copy.107
  32.6 0.5 copy.110
  33.3 0.4 select_reduce_fusion
  33.7 0.2 fusion.2
  34.0 0.4 fusion.3
  34.4 0.2 copy.112
  34.6 0.2 copy.111
  34.9 18.2 %all-gather.1 = f32[128,2,4,66]{3,2,1,0:T(4,128)S(1)} all-gather(f32[8,2,4,66]{3,2,1,0:T(4,128)S(1)} %pad_maximum_fusion), channel_id=3, replica_groups=mesh['seq'=16,'mlp'=8,'tp'=4] {'seq'}, dimensions={0}, use_global_device_ids=true | all-gather | bytes 287232 | tf_op jit(solution)/shard_map/softmax_merge/all_gather | solution.py:141
  53.3 0.3 fusion.23
  53.5 0.3 slice-done
  54.1 0.2 multiply_reduce_fusion.2
  54.4 0.5 copy.119
  54.8 0.5 copy.127
  55.4 1.1 maximum_select_fusion.2
  56.6 4.5 %collective-permute-start.1 = (bf16[2,3,256,128]{3,2,1,0:T(8,128)(2,1)S(1)}, bf16[2,3,256,128]{3,2,1,0:T(8,128)(2,1)S(1)}, u32[]{:S(2)}, u32[]{:S(2)}) collective-permute-start(bf16[2,3,256,128]{3,2,1,0:T(8,128)(2,1)S(1)} %maximum_select_fusion.2), channel_id=1, source_target_pairs={{0,8},{4,12},{8,0},{12,4},{16,24},{20,28},{24,16},{28,20},{1,9},{5... | collective-permute-start | bytes 1179656 | tf_op jit(solution)/shard_map/mlp_weight_gather/ppermute | solution.py:41
  61.1 0.2 fusion.10
  61.5 0.3 fusion
  61.8 17.2 %collective-permute-done.1 = bf16[2,3,256,128]{3,2,1,0:T(8,128)(2,1)S(1)} collective-permute-done((bf16[2,3,256,128]{3,2,1,0:T(8,128)(2,1)S(1)}, bf16[2,3,256,128]{3,2,1,0:T(8,128)(2,1)S(1)}, u32[]{:S(2)}, u32[]{:S(2)}) %collective-permute-start.1) | collective-permute-done | bytes 393248 | tf_op jit(solution)/shard_map/mlp_weight_gather/ppermute | solution.py:41
  79.2 6.9 %collective-permute-start.2 = (bf16[4,3,256,128]{3,2,1,0:T(8,128)(2,1)S(1)}, bf16[4,3,256,128]{3,2,1,0:T(8,128)(2,1)S(1)}, u32[]{:S(2)}, u32[]{:S(2)}) collective-permute-start(bf16[4,3,256,128]{3,2,1,0:T(8,128)(2,1)S(1)} %maximum_select_fusion.1), channel_id=1, source_target_pairs={{0,16},{4,20},{8,24},{12,28},{16,0},{20,4},{24,8},{28,12},{1,17},{... | collective-permute-start | bytes 2359304 | tf_op jit(solution)/shard_map/mlp_weight_gather/ppermute | solution.py:41
  86.5 12.4 %all-gather.2 = f32[32,128]{1,0:T(8,128)S(1)} all-gather(f32[8,128]{1,0:T(8,128)S(1)} %fusion.30), channel_id=4, replica_groups=mesh['seq'=16,'mlp'=8,'tp'=4] {'tp'}, dimensions={0}, use_global_device_ids=true | all-gather | bytes 20480 | tf_op jit(solution)/shard_map/output_projection/all_gather | solution.py:167
  98.9 14.5 %all_gather.30 = bf16[8,2048]{1,0:T(8,128)(2,1)S(1)} all-gather(bf16[8,128]{1,0:T(8,128)(2,1)S(1)} %bitcast_reduce_fusion.2), channel_id=1, replica_groups=mesh['seq'=16,'mlp'=8,'tp'=4] {'seq'}, dimensions={1}, use_global_device_ids=true | all-gather | bytes 34816 | tf_op jit(solution)/shard_map/output_projection/all_gather | solution.py:168
  113.5 8.0 %collective-permute-done.2 = bf16[4,3,256,128]{3,2,1,0:T(8,128)(2,1)S(1)} collective-permute-done((bf16[4,3,256,128]{3,2,1,0:T(8,128)(2,1)S(1)}, bf16[4,3,256,128]{3,2,1,0:T(8,128)(2,1)S(1)}, u32[]{:S(2)}, u32[]{:S(2)}) %collective-permute-start.2) | collective-permute-done | bytes 786464 | tf_op jit(solution)/shard_map/mlp_weight_gather/ppermute | solution.py:41
  121.5 0.2 maximum_select_fusion
  121.9 0.2 reshape_squeeze.11
  122.0 0.3 copy.121
  122.3 0.2 fusion.19
  122.6 0.4 fusion.13
  123.0 12.6 %all-gather.3 = f32[32,2048]{1,0:T(8,128)S(1)} all-gather(f32[8,2048]{1,0:T(8,128)S(1)} %fusion.13), channel_id=5, replica_groups=mesh['seq'=16,'mlp'=8,'tp'=4] {'tp'}, dimensions={0}, use_global_device_ids=true | all-gather | bytes 327680 | tf_op jit(solution)/shard_map/down_reduction/all_gather | solution.py:32
  135.6 1.9 %collective-permute-start.3 = (f32[8,2048]{1,0:T(8,128)S(1)}, f32[8,2048]{1,0:T(8,128)S(1)}, u32[]{:S(2)}, u32[]{:S(2)}) collective-permute-start(f32[8,2048]{1,0:T(8,128)S(1)} %bitcast_reduce_fusion.1), channel_id=1, source_target_pairs={{0,32},{32,0},{64,96},{96,64},{128,160},{160,128},{192,224},{224,1... | collective-permute-start | bytes 196616 | tf_op jit(solution)/shard_map/down_reduction/ppermute | solution.py:55
  137.6 1.2 collective-permute-done.3
  138.8 2.3 %collective-permute-start.4 = (f32[8,2048]{1,0:T(8,128)S(1)}, f32[8,2048]{1,0:T(8,128)S(1)}, u32[]{:S(2)}, u32[]{:S(2)}) collective-permute-start(f32[8,2048]{1,0:T(8,128)S(1)} %add.96), channel_id=1, source_target_pairs={{0,64},{32,96},{64,0},{96,32},{128,192},{160,224},{192,128},{224,1... | collective-permute-start | bytes 196616 | tf_op jit(solution)/shard_map/down_reduction/ppermute | solution.py:55
  141.1 3.9 %collective-permute-done.4 = f32[8,2048]{1,0:T(8,128)S(1)} collective-permute-done((f32[8,2048]{1,0:T(8,128)S(1)}, f32[8,2048]{1,0:T(8,128)S(1)}, u32[]{:S(2)}, u32[]{:S(2)}) %collective-permute-start.4) | collective-permute-done | bytes 65568 | tf_op jit(solution)/shard_map/down_reduction/ppermute | solution.py:55
  145.0 2.2 %collective-permute-start.5 = (f32[8,2048]{1,0:T(8,128)S(1)}, f32[8,2048]{1,0:T(8,128)S(1)}, u32[]{:S(2)}, u32[]{:S(2)}) collective-permute-start(f32[8,2048]{1,0:T(8,128)S(1)} %add.97), channel_id=1, source_target_pairs={{0,128},{32,160},{64,192},{96,224},{128,0},{160,32},{192,64},{224,... | collective-permute-start | bytes 196616 | tf_op jit(solution)/shard_map/down_reduction/ppermute | solution.py:55
  147.1 4.9 %collective-permute-done.5 = f32[8,2048]{1,0:T(8,128)S(1)} collective-permute-done((f32[8,2048]{1,0:T(8,128)S(1)}, f32[8,2048]{1,0:T(8,128)S(1)}, u32[]{:S(2)}, u32[]{:S(2)}) %collective-permute-start.5) | collective-permute-done | bytes 65568 | tf_op jit(solution)/shard_map/down_reduction/ppermute | solution.py:55
  152.0 3.4 %collective-permute-start.6 = (f32[8,2048]{1,0:T(8,128)S(1)}, f32[8,2048]{1,0:T(8,128)S(1)}, u32[]{:S(2)}, u32[]{:S(2)}) collective-permute-start(f32[8,2048]{1,0:T(8,128)S(1)} %add.98), channel_id=1, source_target_pairs={{0,256},{32,288},{64,320},{96,352},{128,384},{160,416},{192,448},{... | collective-permute-start | bytes 196616 | tf_op jit(solution)/shard_map/down_reduction/ppermute | solution.py:55
  155.4 0.7 convert_element_type.88
  156.1 6.7 %collective-permute-done.6 = f32[8,2048]{1,0:T(8,128)S(1)} collective-permute-done((f32[8,2048]{1,0:T(8,128)S(1)}, f32[8,2048]{1,0:T(8,128)S(1)}, u32[]{:S(2)}, u32[]{:S(2)}) %collective-permute-start.6) | collective-permute-done | bytes 65568 | tf_op jit(solution)/shard_map/down_reduction/ppermute | solution.py:55
  162.8 0.6 add_convert_fusion
  (60 shorter events, 2.0 us)
Async XLA Ops:
  0.6 7.8 %copy-start = (bf16[128,512]{1,0:T(8,128)(2,1)S(1)}, bf16[128,512]{1,0:T(8,128)(2,1)}, u32[]{:S(2)}) copy-start(bf16[128,512]{1,0:T(8,128)(2,1)} %param.16) | copy-start | bytes 393220
  0.6 31.3 %copy-start.9 = (s32[8]{0:T(128)S(1)}, s32[8]{0:T(128)}, u32[]{:S(2)}) copy-start(s32[8]{0:T(128)} %param.14) | copy-start | bytes 100
  0.7 31.4 %copy-start.2 = (bf16[8,512,128]{2,1,0:T(8,128)(2,1)S(1)}, bf16[8,512,128]{2,1,0:T(8,128)(2,1)}, u32[]{:S(2)}) copy-start(bf16[8,512,128]{2,1,0:T(8,128)(2,1)} %param.19) | copy-start | bytes 3145732
  2.5 52.9 %collective-permute-start = (bf16[1,3,256,128]{3,2,1,0:T(8,128)(2,1)S(1)}, bf16[1,3,256,128]{3,2,1,0:T(8,128)(2,1)}, u32[]{:S(2)}, u32[]{:S(2)}) collective-permute-start(bf16[1,3,256,128]{3,2,1,0:T(8,128)(2,1)S(1)} %maximum_bitcast_fusion), channel_id=1, source_target_pairs={{0,4},{4,0},{8,12},{12,8},{16,20},{20,16},{24,28},{28,24},{1,5},{5... | collective-permute-start | bytes 589832 | tf_op jit(solution)/shard_map/mlp_weight_gather/ppermute | solution.py:41
  9.6 23.0 %copy-start.3 = (bf16[8,512,128]{2,1,0:T(8,128)(2,1)S(1)}, bf16[8,512,128]{2,1,0:T(8,128)(2,1)}, u32[]{:S(2)}) copy-start(bf16[8,512,128]{2,1,0:T(8,128)(2,1)} %param.20) | copy-start | bytes 3145732
  31.8 1.3 copy-start.5
  53.2 0.7 slice-start
  53.8 7.4 %copy-start.6 = (f32[8,768]{1,0:T(8,128)S(1)}, f32[8,768]{1,0:T(8,128)}, u32[]{:S(2)}) copy-start(f32[8,768]{1,0:T(8,128)} %copy-done.5) | copy-start | bytes 73732
  55.4 31.0 %copy-start.8 = (bf16[2048]{0:T(1024)(128)(2,1)S(1)}, bf16[2048]{0:T(1024)(128)(2,1)}, u32[]{:S(2)}) copy-start(bf16[2048]{0:T(1024)(128)(2,1)} %param.22) | copy-start | bytes 12292
  55.4 30.9 %copy-start.4 = (bf16[512,128]{1,0:T(8,128)(2,1)S(1)}, bf16[512,128]{1,0:T(8,128)(2,1)}, u32[]{:S(2)}) copy-start(bf16[512,128]{1,0:T(8,128)(2,1)} %param.21) | copy-start | bytes 393220
  56.5 56.8 %copy-start.1 = (bf16[8,2048]{1,0:T(8,128)(2,1)S(1)}, bf16[8,2048]{1,0:T(8,128)(2,1)}, u32[]{:S(2)}) copy-start(bf16[8,2048]{1,0:T(8,128)(2,1)} %param.13) | copy-start | bytes 98308
  56.6 22.5 %collective-permute-start.1 = (bf16[2,3,256,128]{3,2,1,0:T(8,128)(2,1)S(1)}, bf16[2,3,256,128]{3,2,1,0:T(8,128)(2,1)S(1)}, u32[]{:S(2)}, u32[]{:S(2)}) collective-permute-start(bf16[2,3,256,128]{3,2,1,0:T(8,128)(2,1)S(1)} %maximum_select_fusion.2), channel_id=1, source_target_pairs={{0,8},{4,12},{8,0},{12,4},{16,24},{20,28},{24,16},{28,20},{1,9},{5... | collective-permute-start | bytes 1179656 | tf_op jit(solution)/shard_map/mlp_weight_gather/ppermute | solution.py:41
  61.3 60.5 %copy-start.7 = (bf16[8,128]{1,0:T(8,128)(2,1)}, bf16[8,128]{1,0:T(8,128)(2,1)S(1)}, u32[]{:S(2)}) copy-start(bf16[8,128]{1,0:T(8,128)(2,1)S(1)} %slice.79) | copy-start | bytes 6148
  79.2 42.3 %collective-permute-start.2 = (bf16[4,3,256,128]{3,2,1,0:T(8,128)(2,1)S(1)}, bf16[4,3,256,128]{3,2,1,0:T(8,128)(2,1)S(1)}, u32[]{:S(2)}, u32[]{:S(2)}) collective-permute-start(bf16[4,3,256,128]{3,2,1,0:T(8,128)(2,1)S(1)} %maximum_select_fusion.1), channel_id=1, source_target_pairs={{0,16},{4,20},{8,24},{12,28},{16,0},{20,4},{24,8},{28,12},{1,17},{... | collective-permute-start | bytes 2359304 | tf_op jit(solution)/shard_map/mlp_weight_gather/ppermute | solution.py:41
  135.6 3.1 %collective-permute-start.3 = (f32[8,2048]{1,0:T(8,128)S(1)}, f32[8,2048]{1,0:T(8,128)S(1)}, u32[]{:S(2)}, u32[]{:S(2)}) collective-permute-start(f32[8,2048]{1,0:T(8,128)S(1)} %bitcast_reduce_fusion.1), channel_id=1, source_target_pairs={{0,32},{32,0},{64,96},{96,64},{128,160},{160,128},{192,224},{224,1... | collective-permute-start | bytes 196616 | tf_op jit(solution)/shard_map/down_reduction/ppermute | solution.py:55
  138.8 6.2 %collective-permute-start.4 = (f32[8,2048]{1,0:T(8,128)S(1)}, f32[8,2048]{1,0:T(8,128)S(1)}, u32[]{:S(2)}, u32[]{:S(2)}) collective-permute-start(f32[8,2048]{1,0:T(8,128)S(1)} %add.96), channel_id=1, source_target_pairs={{0,64},{32,96},{64,0},{96,32},{128,192},{160,224},{192,128},{224,1... | collective-permute-start | bytes 196616 | tf_op jit(solution)/shard_map/down_reduction/ppermute | solution.py:55
  145.0 7.1 %collective-permute-start.5 = (f32[8,2048]{1,0:T(8,128)S(1)}, f32[8,2048]{1,0:T(8,128)S(1)}, u32[]{:S(2)}, u32[]{:S(2)}) collective-permute-start(f32[8,2048]{1,0:T(8,128)S(1)} %add.97), channel_id=1, source_target_pairs={{0,128},{32,160},{64,192},{96,224},{128,0},{160,32},{192,64},{224,... | collective-permute-start | bytes 196616 | tf_op jit(solution)/shard_map/down_reduction/ppermute | solution.py:55
  152.0 10.8 %collective-permute-start.6 = (f32[8,2048]{1,0:T(8,128)S(1)}, f32[8,2048]{1,0:T(8,128)S(1)}, u32[]{:S(2)}, u32[]{:S(2)}) collective-permute-start(f32[8,2048]{1,0:T(8,128)S(1)} %add.98), channel_id=1, source_target_pairs={{0,256},{32,288},{64,320},{96,352},{128,384},{160,416},{192,448},{... | collective-permute-start | bytes 196616 | tf_op jit(solution)/shard_map/down_reduction/ppermute | solution.py:55
